TPU v7x, 256 devices: a whole 4x4x8 slice. The times are simulated.
256 devices in a mesh: ctx: 8 (over z), head: 16 (over y, x), req: 2 (over core).
Axes of the slice: x: 4, y: 4, z: 8, core: 2. Of those that a mesh axis runs over, the one named last changes fastest.
Arguments:
- x_in: bfloat16 [2, 8192, 16384], P('req', 'ctx', 'head'), may hold values from -6 to 6
- bc_in: bfloat16 [2, 8192, 4096], P('req', 'ctx'), may hold values from -0.625 to 0.625
- z_in: bfloat16 [2, 8192, 16384], P('req', 'ctx', 'head'), may hold values from -6 to 6
- dt_raw: float32 [2, 256, 8192], P('req', 'head', 'ctx'), may hold values from -6 to 6
- dt_bias: float32 [256], P('head'), may hold values from -3 to 1
- decay_rate: float32 [256], P('head'), may hold values from 1e-06 to 0.05
- skip_gain: float32 [256], P('head'), may hold values from 0.5 to 1.5
- conv_x: float32 [4, 16384], P(None, 'head'), may hold values from -3 to 3
- conv_bc: float32 [4, 4096], replicated, may hold values from -3 to 3
- ssm_pool: float32 [16, 256, 64, 256], P(('ctx', 'req'), 'head'), may hold values from -6 to 6
- conv_pool: float32 [16, 3, 16384], P(('ctx', 'req'), None, 'head'), may hold values from -6 to 6
- bc_cache: float32 [2, 3, 4096], P('req'), may hold values from -0.625 to 0.625
- owner: int32 [2, 16], P(None, 'head'), may hold values from 0 to 15, as said below
- lengths: int32 [2], replicated, may hold values from 2048 to 8192, as said below
Outputs:
- y_out: bfloat16 [2, 8192, 16384], P('req', 'ctx', 'head')
- block_states: float32 [2, 8, 256, 64, 256], P('req', 'ctx', 'head')
Inputs may be any that keep to these rules, and one draw needn't show every extreme that they name: `owner`: for every head block the requests' cached states lie in different slots. `lengths`: one request has all 8192 new tokens.
All inputs are finite; a program needn't handle non-finite values.
Results may differ from a plain program's by a relative error of at most 0.0053.
Values may be sent and summed in bfloat16 or wider, within the bound.
No kernel may reach another device: no remote copies, remote signals or barrier semaphores. Data moves between devices by JAX's collectives and lax.ppermute only.
A program may use at most 128 MiB of HBM per device.

v0:
```python
from functools import partial
import jax
import jax.numpy as jnp
from jax import lax
from jax.sharding import PartitionSpec as P

H = 256
P_SIZE = 64
N = 256
G = 8
K = 4
STRETCH = 256
CHUNKS = 4
HIGHEST = lax.Precision.HIGHEST


def passed_along(value, axis, steps):
    count = lax.axis_size(axis)
    initial, last = (max(0, -steps), min(count, count - steps))
    return lax.ppermute(value, axis, [(source, source + steps) for source in range(initial, last)])


def causal_conv(prev_rows, rows, taps):
    padded = jnp.concatenate([prev_rows, rows.astype(jnp.float32)], axis=0)
    count = rows.shape[0]
    total = taps[0] * padded[0:count]
    for offset in range(1, taps.shape[0]):
        total = total + taps[offset] * padded[offset : offset + count]
    return jax.nn.silu(total).astype(jnp.bfloat16)


def block_state(running, x_blk, b_blk, step_blk, cum):
    block_len, head_count = (x_blk.shape[0], x_blk.shape[1])
    group_count = b_blk.shape[1]
    per_group = head_count // group_count
    block_end = cum[:, -1:]
    factor = step_blk * jnp.exp(-(block_end - cum))
    weighted = (x_blk.astype(jnp.float32) * factor.T[:, :, None]).astype(jnp.bfloat16)
    weighted_view = weighted.reshape(block_len, group_count, per_group, running.shape[1])
    contrib = jnp.einsum(
        "qgjp,qgn->gjpn", weighted_view, b_blk, preferred_element_type=jnp.float32
    ).reshape(running.shape)
    return jnp.exp(-cum[:, -1])[:, None, None] * running + contrib


def block_output(running, x_blk, b_blk, c_blk, step_blk, cum, skip_gain):
    block_len = x_blk.shape[0]
    head_count = x_blk.shape[1]
    scores = jnp.einsum("qgn,sgn->gqs", c_blk, b_blk, preferred_element_type=jnp.float32)
    group_count = scores.shape[0]
    per_group = head_count // group_count
    scores_h = jnp.broadcast_to(
        scores[:, None], (group_count, per_group, block_len, block_len)
    ).reshape(head_count, block_len, block_len)
    row_ids = lax.broadcasted_iota(jnp.int32, (block_len, block_len), 0)
    col_ids = lax.broadcasted_iota(jnp.int32, (block_len, block_len), 1)
    causal = (row_ids >= col_ids)[None]
    decay_gap = jnp.where(causal, cum[:, :, None] - cum[:, None, :], 0.0)
    decay_mask = jnp.where(causal, jnp.exp(-decay_gap), 0.0)
    weights = (scores_h * decay_mask * step_blk[:, None, :]).astype(jnp.bfloat16)
    y_intra = jnp.einsum("hqs,shp->qhp", weights, x_blk, preferred_element_type=jnp.float32)
    state_view = running.reshape(group_count, per_group, running.shape[1], running.shape[2])
    y_state = jnp.einsum("qgn,gjpn->qgjp", c_blk.astype(jnp.float32), state_view, precision=HIGHEST)
    y_state = y_state.reshape(block_len, head_count, running.shape[1]) * jnp.exp(-cum).T[:, :, None]
    return y_intra + y_state + skip_gain[None, :, None] * x_blk.astype(jnp.float32)


def on_device(
    x_in,
    bc_in,
    z_in,
    dt_raw,
    dt_bias,
    decay_rate,
    skip_gain,
    conv_x,
    conv_bc,
    ssm_pool,
    conv_pool,
    bc_cache,
    owner,
    lengths,
):
    n_ctx = lax.axis_size("ctx")
    n_req = lax.axis_size("req")
    ctx_pos = lax.axis_index("ctx")
    head_pos = lax.axis_index("head")
    req_pos = lax.axis_index("req")
    local_heads = dt_raw.shape[1]
    tokens = x_in.shape[1]
    at_start = ctx_pos == 0
    want = owner[req_pos, 0]
    on_chip = want // n_req == ctx_pos
    mine = want % n_req == req_pos
    swap = [(src, n_req - 1 - src) for src in range(n_req)]
    other_pool, other_conv = lax.ppermute((ssm_pool[0], conv_pool[0]), "req", swap)
    state_pick = jnp.where(on_chip, jnp.where(mine, ssm_pool[0], other_pool), 0.0)
    conv_pick = jnp.where(on_chip, jnp.where(mine, conv_pool[0], other_conv), 0.0)
    picked = jnp.concatenate([state_pick.reshape(-1), conv_pick.reshape(-1)])
    picked, x_in, bc_in, dt_raw = lax.optimization_barrier((picked, x_in, bc_in, dt_raw))
    picked = lax.psum(picked, "ctx")
    first_state = picked[: state_pick.size].reshape(state_pick.shape)
    first_conv = picked[state_pick.size :].reshape(conv_pick.shape)
    tail_x = x_in[0, tokens - (K - 1) :, :]
    tail_bc = bc_in[0, tokens - (K - 1) :, :]
    prev_x, prev_bc = passed_along((tail_x, tail_bc), "ctx", 1)
    prev_x = jnp.where(at_start, first_conv, prev_x.astype(jnp.float32))
    prev_bc = jnp.where(at_start, bc_cache[0], prev_bc.astype(jnp.float32))
    per_group = H // G
    local_groups = max(1, local_heads // per_group)
    group_start = head_pos * local_heads // per_group
    span = local_groups * N

    def pick_groups(values):
        input_cols = lax.dynamic_slice_in_dim(values, group_start * N, span, 1)
        output_cols = lax.dynamic_slice_in_dim(values, G * N + group_start * N, span, 1)
        return jnp.concatenate([input_cols, output_cols], axis=1)

    x_head = causal_conv(prev_x, x_in[0, : K - 1], conv_x)
    x_rest = causal_conv(x_in[0, : K - 1].astype(jnp.float32), x_in[0, K - 1 :], conv_x)
    x_conv = jnp.concatenate([x_head, x_rest], axis=0)
    bc_conv = causal_conv(pick_groups(prev_bc), pick_groups(bc_in[0]), pick_groups(conv_bc))
    positions = ctx_pos * tokens + lax.iota(jnp.int32, tokens)
    live_mask = (positions < lengths[req_pos]).astype(jnp.float32)
    step_size = jax.nn.softplus(dt_raw[0] + dt_bias[:, None]) * live_mask[None, :]
    log_decay = step_size * decay_rate[:, None]
    blocks = tokens // STRETCH
    x_view = x_conv.reshape(blocks, STRETCH, local_heads, P_SIZE)
    b_view = bc_conv[:, :span].reshape(blocks, STRETCH, local_groups, N)
    c_view = bc_conv[:, span:].reshape(blocks, STRETCH, local_groups, N)
    step_view = step_size.reshape(local_heads, blocks, STRETCH).transpose(1, 0, 2)
    log_view = log_decay.reshape(local_heads, blocks, STRETCH).transpose(1, 0, 2)
    cum_view = jnp.cumsum(log_view, axis=2)
    running = jnp.zeros((local_heads, P_SIZE, N), jnp.float32)
    starts = []
    for blk in range(blocks):
        starts.append(running)
        running = block_state(running, x_view[blk], b_view[blk], step_view[blk], cum_view[blk])
    local_end = running
    own_decay = jnp.exp(-jnp.sum(log_decay, axis=1))
    chunk = local_heads // CHUNKS
    end_chunks = local_end.reshape(CHUNKS, chunk, P_SIZE, N)
    init_chunks = first_state.reshape(CHUNKS, chunk, P_SIZE, N)
    decay_chunks = own_decay.reshape(CHUNKS, chunk)
    got = jnp.zeros((chunk, P_SIZE, N), jnp.float32)
    received = []
    for step in range(n_ctx + CHUNKS - 2):
        index = jnp.clip(step - ctx_pos, 0, CHUNKS - 1)
        prior = jnp.where(
            at_start, lax.dynamic_index_in_dim(init_chunks, index, keepdims=False), got
        )
        sent = lax.dynamic_index_in_dim(decay_chunks, index, keepdims=False)[
            :, None, None
        ] * prior + lax.dynamic_index_in_dim(end_chunks, index, keepdims=False)
        pairs = [
            (src, src + 1) for src in range(max(0, step - CHUNKS + 1), min(step, n_ctx - 2) + 1)
        ]
        got = lax.ppermute(sent, "ctx", pairs)
        received.append(got)
    received = jnp.stack(received)
    prefix = lax.dynamic_slice_in_dim(received, jnp.maximum(ctx_pos - 1, 0), CHUNKS, 0)
    start_state = jnp.where(at_start, first_state, prefix.reshape(local_heads, P_SIZE, N))
    end_state = own_decay[:, None, None] * start_state + local_end
    outs = []
    for blk in range(blocks):
        outs.append(
            block_output(
                starts[blk],
                x_view[blk],
                b_view[blk],
                c_view[blk],
                step_view[blk],
                cum_view[blk],
                skip_gain,
            )
        )
    local_out = jnp.concatenate(outs, axis=0)
    cum_dev = jnp.cumsum(log_decay, axis=1)
    readout = bc_conv[:, span:].reshape(tokens, local_groups, N)
    start_view = start_state.reshape(local_groups, local_heads // local_groups, P_SIZE, N)
    carried = jnp.einsum(
        "tgn,gjpn->tgjp", readout.astype(jnp.float32), start_view, precision=HIGHEST
    )
    carried = carried.reshape(tokens, local_heads, P_SIZE) * jnp.exp(-cum_dev).T[:, :, None]
    mixed = local_out + carried
    gate_act = jax.nn.silu(z_in[0].astype(jnp.float32)).reshape(tokens, local_heads, P_SIZE)
    gated = (
        (mixed * gate_act * live_mask[:, None, None])
        .reshape(1, tokens, local_heads * P_SIZE)
        .astype(jnp.bfloat16)
    )
    return (gated, end_state[None, None])


def solution(mesh):
    return jax.shard_map(
        on_device,
        mesh=mesh,
        in_specs=(
            P("req", "ctx", "head"),
            P("req", "ctx", None),
            P("req", "ctx", "head"),
            P("req", "head", "ctx"),
            P("head"),
            P("head"),
            P("head"),
            P(None, "head"),
            P(),
            P(("ctx", "req"), "head", None, None),
            P(("ctx", "req"), None, "head"),
            P("req", None, None),
            P(None, "head"),
            P(),
        ),
        out_specs=(P("req", "ctx", "head"), P("req", "ctx", "head", None, None)),
        check_vma=False,
    )
```

profile of v0, /device:TPU:232, one launch (start us, length us, event | category | flops | bytes accessed | tf_op | source)
XLA Modules:
  0.0 251.9 jit_solution(4440000627590166594)
XLA Ops:
  8.6 1.2 dynamic_slice.132
  13.1 1.5 fusion.151
  14.6 1.2 fusion.127
  19.1 3.9 %copy.78 = bf16[1,1024,1024]{1,2,0:T(8,128)(2,1)} copy(bf16[1,1024,1024]{2,1,0:T(8,128)(2,1)} %param.16) | data formatting | bytes 4194304 | tf_op args[2]
  23.8 1.1 pad_maximum_fusion.2
  24.9 1.3 dynamic-slice_bitcast_fusion.1
  26.2 1.6 slice_bitcast_fusion.3
  27.7 2.9 %copy.66 = bf16[1,1024,1024]{1,2,0:T(8,128)(2,1)S(1)} copy(bf16[1,1024,1024]{2,1,0:T(8,128)(2,1)} %param.14) | data formatting | bytes 4194304 | tf_op jit(solution)/shard_map/optimization_barrier | solution.py:100
  30.6 1.3 slice_bitcast_fusion.4
  32.2 2.3 reduce-window.14
  41.4 1.3 collective-permute-start.3
  42.7 3.0 %fusion.21 = f32[1021,1024]{0,1:T(8,128)} fusion(bf16[1,1024,1024]{1,2,0:T(8,128)(2,1)S(1)} %copy.66), kind=kLoop, calls=%fused_computation.38 | loop fusion | flops 1045504 | bytes 6273024 | tf_op jit(solution)/shard_map/convert_element_type | solution.py:24
  46.7 1.5 collective-permute-start.2
  48.2 11.3 %multiply_convert_fusion.4 = bf16[1021,1024]{0,1:T(8,128)(2,1)S(1)} fusion(f32[1021,1024]{0,1:T(8,128)} %fusion.21, f32[3,1024]{0,1:T(8,128)} %copy.67, f32[1024]{0:T(1024)S(1)} %bitcast.440, f32[1024]{0:T(1024)S(1)} %bitcast.442, f32[1024]{0:T(1024)S(1)} %bitcast.438, f32[1024]{0:T(1024)S(1)} %bitcast.436), kind=kLoop, calls=%fused_computation.24 | loop fusion | flops 15682560 | bytes 6301696 | tf_op jit(solution)/shard_map/convert_element_type | solution.py:29
  59.5 1.9 fusion.148
  62.4 4.5 %reduce-window.16 = f32[16,8,128]{2,1,0:T(8,128)S(1)} reduce-window(f32[16,8,128]{2,1,0:T(8,128)S(1)} %fusion.116, f32[]{:T(128)} %constant.162.clone.1), window={size=1x1x128 pad=0_0x0_0x127_0}, to_apply=%region_4.5 | reduce-window | flops 2080768 | bytes 131076 | tf_op jit(solution)/shard_map/reduce-window.2
  67.4 1.6 maximum_convert_fusion
  72.3 1.9 pad_maximum_fusion.1
  74.2 1.2 multiply_convert_fusion.9
  75.5 1.1 fusion.102
  76.5 50.6 %all-reduce.2.cloned.1.call-done = f32[265216]{0:T(1024)} async-done(((f32[265216]{0:T(1024)}), f32[265216]{0:T(1024)}) %all-reduce.2.cloned.1.call-update) | async-done | bytes 1060880 | tf_op jit(solution)/shard_map/psum | solution.py:101
  129.4 2.9 %fusion.65 = (bf16[256,1024]{0,1:T(8,128)(2,1)S(1)}, bf16[256,1024]{0,1:T(8,128)(2,1)}, bf16[256,1024]{0,1:T(8,128)(2,1)S(1)}, bf16[256,1024]{0,1:T(8,128)(2,1)S(1)}, bf16[256,1024]{0,1:T(8,128)(2,1)S(1)}) fusion(f32[256,16]{0,1:T(8,128)S(1)} %get-tuple-element.52, bf16[1021,1024]{0,1:T(8,128)(2,1)S(1)} %multiply_convert_fusion.4, ...), kind=kLoop, calls=%fused_computation.94 | loop fusion | flops 4194304 | bytes 6619136 | tf_op jit(solution)/shard_map/convert_element_type | solution.py:38
  132.6 1.3 fusion.85
  134.2 1.3 fusion.79
  135.6 1.3 reshape_reshape.3
  137.0 2.1 multiply_add_fusion
  140.0 1.4 fusion.48
  142.5 2.6 %fusion.47 = f32[256,16,64]{0,2,1:T(8,128)} fusion(bf16[256,16,64]{0,2,1:T(8,128)(2,1)S(1)} %bitcast.410, f32[16,256]{1,0:T(8,128)S(1)} %copy-done.54, f32[16,256]{1,0:T(8,128)S(1)} %bitcast.433, f32[256,256]{1,0:T(8,128)S(1)} %fusion.97, pred[256,256]{1,0:T(8,128)(4,1)S(1)} %copy-done.37), kind=kOutput, calls=%fused_computation.65 | convolution fusion | flops 141557760 | bytes 1933312 | tf_op jit(solution)/shard_map/hqs,shp->qhp/dot_general | solution.py:61
  146.4 2.6 %fusion.46 = f32[256,16,64]{0,2,1:T(8,128)} fusion(bf16[256,16,64]{0,2,1:T(8,128)(2,1)S(1)} %bitcast.414, f32[16,256]{1,0:T(8,128)S(1)} %copy-done.52, f32[16,256]{1,0:T(8,128)S(1)} %bitcast.429, f32[256,256]{1,0:T(8,128)S(1)} %fusion.92, pred[256,256]{1,0:T(8,128)(4,1)S(1)} %copy-done.37), kind=kOutput, calls=%fused_computation.64 | convolution fusion | flops 141557760 | bytes 1933312 | tf_op jit(solution)/shard_map/hqs,shp->qhp/dot_general | solution.py:61
  150.1 1.4 fusion.49
  152.3 1.8 fusion.59
  155.0 1.4 collective-permute-start.9
  156.4 1.7 fusion.58
  158.0 2.5 slice.267
  160.6 1.2 bitcast_add_fusion.3
  161.8 1.3 collective-permute-start.10
  165.1 42.8 %collective-permute-done.10 = f32[4,64,256]{2,1,0:T(8,128)S(1)} collective-permute-done((f32[4,64,256]{2,1,0:T(8,128)S(1)}, f32[4,64,256]{2,1,0:T(8,128)S(1)}, u32[]{:S(2)}, u32[]{:S(2)}) %collective-permute-start.10) | collective-permute-done | bytes 262176 | tf_op jit(solution)/shard_map/ppermute | solution.py:158
  207.9 1.0 bitcast_add_fusion.2
  209.0 1.6 collective-permute-start.11
  211.6 6.3 %collective-permute-done.11 = f32[4,64,256]{2,1,0:T(8,128)S(1)} collective-permute-done((f32[4,64,256]{2,1,0:T(8,128)S(1)}, f32[4,64,256]{2,1,0:T(8,128)S(1)}, u32[]{:S(2)}, u32[]{:S(2)}) %collective-permute-start.11) | collective-permute-done | bytes 262176 | tf_op jit(solution)/shard_map/ppermute | solution.py:158
  218.0 1.3 collective-permute-start.12
  220.3 6.0 %collective-permute-done.12 = f32[4,64,256]{2,1,0:T(8,128)S(1)} collective-permute-done((f32[4,64,256]{2,1,0:T(8,128)S(1)}, f32[4,64,256]{2,1,0:T(8,128)S(1)}, u32[]{:S(2)}, u32[]{:S(2)}) %collective-permute-start.12) | collective-permute-done | bytes 262176 | tf_op jit(solution)/shard_map/ppermute | solution.py:158
  226.4 1.3 collective-permute-start.13
  227.8 6.9 %collective-permute-done.13 = f32[4,64,256]{2,1,0:T(8,128)S(1)} collective-permute-done((f32[4,64,256]{2,1,0:T(8,128)S(1)}, f32[4,64,256]{2,1,0:T(8,128)S(1)}, u32[]{:S(2)}, u32[]{:S(2)}) %collective-permute-start.13) | collective-permute-done | bytes 262176 | tf_op jit(solution)/shard_map/ppermute | solution.py:158
  234.9 1.6 add_bitcast_fusion
  236.5 1.8 fusion.67
  240.6 1.9 fusion.13
  242.5 2.6 %copy.79 = bf16[1,1024,1024]{2,1,0:T(8,128)(2,1)} copy(bf16[1,1024,1024]{1,2,0:T(8,128)(2,1)S(1)} %fusion.13) | data formatting | bytes 4194304
  (282 shorter events, 33.6 us)
Async XLA Ops:
  7.2 8.6 %copy-start = (s32[2,1]{0,1:T(1,128)S(1)}, s32[2,1]{0,1:T(1,128)}, u32[]{:S(2)}) copy-start(s32[2,1]{0,1:T(1,128)} %param.26) | copy-start | bytes 28
  7.2 15.9 %copy-start.30 = (f32[1,16,64,256]{3,2,1,0:T(8,128)S(1)}, f32[1,16,64,256]{3,2,1,0:T(8,128)}, u32[]{:S(2)}) copy-start(f32[1,16,64,256]{3,2,1,0:T(8,128)} %param.23) | copy-start | bytes 3145732
  7.2 15.8 %copy-start.38 = (f32[1,3,1024]{2,0,1:T(1,128)S(1)}, f32[1,3,1024]{2,0,1:T(1,128)}, u32[]{:S(2)}) copy-start(f32[1,3,1024]{2,0,1:T(1,128)} %param.24) | copy-start | bytes 36868
  7.2 119.9 %all-reduce.2.cloned.1.call-start = ((), (), s32[]{:S(2)}) async-start(), calls=%async_computation | async-start | bytes 2121728 | tf_op jit(solution)/shard_map/psum | solution.py:101
  7.2 15.8 %collective-permute-start = (f32[16,64,256]{2,1,0:T(8,128)}, f32[16,64,256]{2,1,0:T(8,128)S(1)}, u32[]{:S(2)}, u32[]{:S(2)}) collective-permute-start(f32[16,64,256]{2,1,0:T(8,128)} %bitcast.416), channel_id=1, source_target_pairs={{0,1},{1,0},{2,3},{3,2},{4,5},{5,4},{6,7},{7,6},{8,9},{9,8},{10,11... | collective-permute-start | bytes 3145736 | tf_op jit(solution)/shard_map/ppermute | solution.py:96
  8.1 14.9 %collective-permute-start.1 = (f32[3,1024]{1,0:T(4,128)S(1)}, f32[3,1024]{1,0:T(4,128)S(1)}, u32[]{:S(2)}, u32[]{:S(2)}) collective-permute-start(f32[3,1024]{1,0:T(4,128)S(1)} %bitcast.445), channel_id=1, source_target_pairs={{0,1},{1,0},{2,3},{3,2},{4,5},{5,4},{6,7},{7,6},{8,9},{9,8},{10,11... | collective-permute-start | bytes 36872 | tf_op jit(solution)/shard_map/ppermute | solution.py:96
  23.7 8.2 %copy-start.33 = (f32[1,16,1024]{2,1,0:T(8,128)S(1)}, f32[1,16,1024]{2,1,0:T(8,128)}, u32[]{:S(2)}) copy-start(f32[1,16,1024]{2,1,0:T(8,128)} %param.17) | copy-start | bytes 196612
  23.8 8.2 %copy-start.64 = (f32[16]{0:T(128)S(1)}, f32[16]{0:T(128)}, u32[]{:S(2)}) copy-start(f32[16]{0:T(128)} %param.18) | copy-start | bytes 196
  23.8 8.2 %copy-start.66 = (f32[16]{0:T(128)S(1)}, f32[16]{0:T(128)}, u32[]{:S(2)}) copy-start(f32[16]{0:T(128)} %param.19) | copy-start | bytes 196
  26.1 41.2 %copy-start.11 = (bf16[1024,256]{1,0:T(8,128)(2,1)}, bf16[1024,256]{1,0:T(8,128)(2,1)S(1)}, u32[]{:S(2)}) copy-start(bf16[1024,256]{1,0:T(8,128)(2,1)S(1)} %get-tuple-element.27) | copy-start | bytes 1572868
  26.2 41.2 %copy-start.13 = (bf16[1024,256]{1,0:T(8,128)(2,1)}, bf16[1024,256]{1,0:T(8,128)(2,1)S(1)}, u32[]{:S(2)}) copy-start(bf16[1024,256]{1,0:T(8,128)(2,1)S(1)} %get-tuple-element.28) | copy-start | bytes 1572868
  36.8 11.4 %copy-start.48 = (f32[1,1024]{1,0:T(1,128)S(1)}, f32[1,1024]{1,0:T(1,128)}, u32[]{:S(2)}) copy-start(f32[1,1024]{1,0:T(1,128)} %get-tuple-element.61) | copy-start | bytes 12292
  36.8 11.4 %copy-start.49 = (f32[1,1024]{1,0:T(1,128)S(1)}, f32[1,1024]{1,0:T(1,128)}, u32[]{:S(2)}) copy-start(f32[1,1024]{1,0:T(1,128)} %get-tuple-element.62) | copy-start | bytes 12292
  41.4 30.8 %collective-permute-start.3 = (bf16[3,4096]{1,0:T(4,128)(2,1)}, bf16[3,4096]{1,0:T(4,128)(2,1)S(1)}, u32[]{:S(2)}, u32[]{:S(2)}) collective-permute-start(bf16[3,4096]{1,0:T(4,128)(2,1)} %slice_bitcast_fusion.3), channel_id=1, source_target_pairs={{0,32},{32,64},{64,96},{96,128},{128,160},{160,192},{192,224},{1,3... | collective-permute-start | bytes 73736 | tf_op jit(solution)/shard_map/ppermute | solution.py:20
  46.7 81.2 %collective-permute-start.2 = (bf16[3,1024]{1,0:T(4,128)(2,1)}, bf16[3,1024]{1,0:T(4,128)(2,1)S(1)}, u32[]{:S(2)}, u32[]{:S(2)}) collective-permute-start(bf16[3,1024]{1,0:T(4,128)(2,1)} %get-tuple-element.35), channel_id=1, source_target_pairs={{0,32},{32,64},{64,96},{96,128},{128,160},{160,192},{192,224},{1,3... | collective-permute-start | bytes 18440 | tf_op jit(solution)/shard_map/ppermute | solution.py:20
  48.2 13.2 %copy-start.65 = (f32[16]{0:T(128)S(1)}, f32[16]{0:T(128)}, u32[]{:S(2)}) copy-start(f32[16]{0:T(128)} %param.18) | copy-start | bytes 196
  48.2 13.2 %copy-start.67 = (f32[16]{0:T(128)S(1)}, f32[16]{0:T(128)}, u32[]{:S(2)}) copy-start(f32[16]{0:T(128)} %param.19) | copy-start | bytes 196
  48.2 14.1 %copy-start.50 = (f32[8,128]{1,0:T(8,128)S(1)}, f32[8,128]{1,0:T(8,128)}, u32[]{:S(2)}) copy-start(f32[8,128]{1,0:T(8,128)} %fusion.127) | copy-start | bytes 12292
  59.5 12.7 %copy-start.39 = (f32[1,3,4096]{2,0,1:T(1,128)S(1)}, f32[1,3,4096]{2,0,1:T(1,128)}, u32[]{:S(2)}) copy-start(f32[1,3,4096]{2,0,1:T(1,128)} %param.25) | copy-start | bytes 147460
  62.3 11.9 %copy-start.59 = (f32[1,512]{1,0:T(1,128)S(1)}, f32[1,512]{1,0:T(1,128)}, u32[]{:S(2)}) copy-start(f32[1,512]{1,0:T(1,128)} %get-tuple-element.63) | copy-start | bytes 6148
  62.3 11.9 %copy-start.60 = (f32[1,512]{1,0:T(1,128)S(1)}, f32[1,512]{1,0:T(1,128)}, u32[]{:S(2)}) copy-start(f32[1,512]{1,0:T(1,128)} %get-tuple-element.64) | copy-start | bytes 6148
  62.3 11.9 %copy-start.61 = (f32[1,512]{1,0:T(1,128)S(1)}, f32[1,512]{1,0:T(1,128)}, u32[]{:S(2)}) copy-start(f32[1,512]{1,0:T(1,128)} %get-tuple-element.65) | copy-start | bytes 6148
  62.3 11.9 %copy-start.62 = (f32[1,512]{1,0:T(1,128)S(1)}, f32[1,512]{1,0:T(1,128)}, u32[]{:S(2)}) copy-start(f32[1,512]{1,0:T(1,128)} %get-tuple-element.66) | copy-start | bytes 6148
  75.4 58.8 %copy-start.4 = (bf16[1024,512]{1,0:T(8,128)(2,1)}, bf16[1024,512]{1,0:T(8,128)(2,1)S(1)}, u32[]{:S(2)}) copy-start(bf16[1024,512]{1,0:T(8,128)(2,1)S(1)} %multiply_convert_fusion.9) | copy-start | bytes 3145732
  139.2 2.4 collective-permute-start.4
  141.7 3.5 %collective-permute-start.5 = (f32[4,64,256]{2,1,0:T(8,128)S(1)}, f32[4,64,256]{2,1,0:T(8,128)S(1)}, u32[]{:S(2)}, u32[]{:S(2)}) collective-permute-start(f32[4,64,256]{2,1,0:T(8,128)S(1)} %bitcast_add_fusion.8), channel_id=1, source_target_pairs={{0,32},{32,64},{1,33},{33,65},{2,34},{34,66},{3,35},{35,67},{4,36}... | collective-permute-start | bytes 786440 | tf_op jit(solution)/shard_map/ppermute | solution.py:158
  145.4 3.8 %collective-permute-start.6 = (f32[4,64,256]{2,1,0:T(8,128)S(1)}, f32[4,64,256]{2,1,0:T(8,128)S(1)}, u32[]{:S(2)}, u32[]{:S(2)}) collective-permute-start(f32[4,64,256]{2,1,0:T(8,128)S(1)} %bitcast_add_fusion.7), channel_id=1, source_target_pairs={{0,32},{32,64},{64,96},{1,33},{33,65},{65,97},{2,34},{34,66},{66,9... | collective-permute-start | bytes 786440 | tf_op jit(solution)/shard_map/ppermute | solution.py:158
  149.3 2.2 collective-permute-start.7
  151.6 2.5 %collective-permute-start.8 = (f32[4,64,256]{2,1,0:T(8,128)S(1)}, f32[4,64,256]{2,1,0:T(8,128)S(1)}, u32[]{:S(2)}, u32[]{:S(2)}) collective-permute-start(f32[4,64,256]{2,1,0:T(8,128)S(1)} %bitcast_add_fusion.5), channel_id=1, source_target_pairs={{32,64},{64,96},{96,128},{128,160},{33,65},{65,97},{97,129},{129,1... | collective-permute-start | bytes 786440 | tf_op jit(solution)/shard_map/ppermute | solution.py:158
  152.3 8.3 %copy-start.74 = (f32[4]{0:T(128)S(1)}, f32[4]{0:T(128)}, u32[]{:S(2)}) copy-start(f32[4]{0:T(128)} %get-tuple-element.70) | copy-start | bytes 52
  154.2 53.8 %copy-start.73 = (f32[4]{0:T(128)S(1)}, f32[4]{0:T(128)}, u32[]{:S(2)}) copy-start(f32[4]{0:T(128)} %get-tuple-element.69) | copy-start | bytes 52
  155.0 5.6 %collective-permute-start.9 = (f32[4,64,256]{2,1,0:T(8,128)}, f32[4,64,256]{2,1,0:T(8,128)}, u32[]{:S(2)}, u32[]{:S(2)}) collective-permute-start(f32[4,64,256]{2,1,0:T(8,128)} %bitcast_add_fusion.4), channel_id=1, source_target_pairs={{64,96},{96,128},{128,160},{160,192},{65,97},{97,129},{129,161},{1... | collective-permute-start | bytes 786440 | tf_op jit(solution)/shard_map/ppermute | solution.py:158
  156.3 61.6 %copy-start.72 = (f32[4]{0:T(128)S(1)}, f32[4]{0:T(128)}, u32[]{:S(2)}) copy-start(f32[4]{0:T(128)} %get-tuple-element.68) | copy-start | bytes 52
  158.0 68.3 %copy-start.71 = (f32[4]{0:T(128)S(1)}, f32[4]{0:T(128)}, u32[]{:S(2)}) copy-start(f32[4]{0:T(128)} %get-tuple-element.67) | copy-start | bytes 52
  160.5 51.0 %copy-start.29 = (f32[4,64,256]{2,1,0:T(8,128)S(1)}, f32[4,64,256]{2,1,0:T(8,128)}, u32[]{:S(2)}) copy-start(f32[4,64,256]{2,1,0:T(8,128)} %copy-done.28) | copy-start | bytes 786436
  160.6 57.4 %copy-start.3 = (f32[4,4,64,256]{3,2,1,0:T(8,128)S(1)}, f32[4,4,64,256]{3,2,1,0:T(8,128)}, u32[]{:S(2)}) copy-start(f32[4,4,64,256]{3,2,1,0:T(8,128)} %reshape_reshape.3) | copy-start | bytes 3145732
  161.8 46.1 %collective-permute-start.10 = (f32[4,64,256]{2,1,0:T(8,128)S(1)}, f32[4,64,256]{2,1,0:T(8,128)S(1)}, u32[]{:S(2)}, u32[]{:S(2)}) collective-permute-start(f32[4,64,256]{2,1,0:T(8,128)S(1)} %bitcast_add_fusion.3), channel_id=1, source_target_pairs={{96,128},{128,160},{160,192},{192,224},{97,129},{129,161},{161,193... | collective-permute-start | bytes 786440 | tf_op jit(solution)/shard_map/ppermute | solution.py:158
  208.9 25.8 %copy-start.8 = (f32[16,64,256]{2,1,0:T(8,128)S(1)}, f32[16,64,256]{2,1,0:T(8,128)}, u32[]{:S(2)}) copy-start(f32[16,64,256]{2,1,0:T(8,128)} %fusion.85) | copy-start | bytes 3145732
  209.0 25.8 %copy-start.9 = (f32[16,64,256]{2,1,0:T(8,128)S(1)}, f32[16,64,256]{2,1,0:T(8,128)}, u32[]{:S(2)}) copy-start(f32[16,64,256]{2,1,0:T(8,128)} %fusion.79) | copy-start | bytes 3145732
  209.0 25.8 %copy-start.17 = (f32[16,64,256]{2,1,0:T(8,128)S(1)}, f32[16,64,256]{2,1,0:T(8,128)}, u32[]{:S(2)}) copy-start(f32[16,64,256]{2,1,0:T(8,128)} %slice.267) | copy-start | bytes 3145732
  209.0 25.8 %copy-start.70 = (f32[16]{0:T(128)S(1)}, f32[16]{0:T(128)}, u32[]{:S(2)}) copy-start(f32[16]{0:T(128)} %copy-done.69) | copy-start | bytes 196
  209.0 25.8 %copy-start.80 = (f32[16]{0:T(128)S(1)}, f32[16]{0:T(128)}, u32[]{:S(2)}) copy-start(f32[16]{0:T(128)} %get-tuple-element.83) | copy-start | bytes 196
  209.0 25.8 %copy-start.81 = (f32[16]{0:T(128)S(1)}, f32[16]{0:T(128)}, u32[]{:S(2)}) copy-start(f32[16]{0:T(128)} %get-tuple-element.84) | copy-start | bytes 196
  209.0 25.8 %copy-start.83 = (f32[16]{0:T(128)S(1)}, f32[16]{0:T(128)}, u32[]{:S(2)}) copy-start(f32[16]{0:T(128)} %negate_exponential_fusion.3) | copy-start | bytes 196
  209.0 8.9 %collective-permute-start.11 = (f32[4,64,256]{2,1,0:T(8,128)S(1)}, f32[4,64,256]{2,1,0:T(8,128)S(1)}, u32[]{:S(2)}, u32[]{:S(2)}) collective-permute-start(f32[4,64,256]{2,1,0:T(8,128)S(1)} %bitcast_add_fusion.2), channel_id=1, source_target_pairs={{128,160},{160,192},{192,224},{129,161},{161,193},{193,225},{130,1... | collective-permute-start | bytes 786440 | tf_op jit(solution)/shard_map/ppermute | solution.py:158
  218.0 8.3 %collective-permute-start.12 = (f32[4,64,256]{2,1,0:T(8,128)S(1)}, f32[4,64,256]{2,1,0:T(8,128)S(1)}, u32[]{:S(2)}, u32[]{:S(2)}) collective-permute-start(f32[4,64,256]{2,1,0:T(8,128)S(1)} %bitcast_add_fusion.1), channel_id=1, source_target_pairs={{160,192},{192,224},{161,193},{193,225},{162,194},{194,226},{163,1... | collective-permute-start | bytes 786440 | tf_op jit(solution)/shard_map/ppermute | solution.py:158
  226.4 8.3 %collective-permute-start.13 = (f32[4,64,256]{2,1,0:T(8,128)S(1)}, f32[4,64,256]{2,1,0:T(8,128)S(1)}, u32[]{:S(2)}, u32[]{:S(2)}) collective-permute-start(f32[4,64,256]{2,1,0:T(8,128)S(1)} %bitcast_add_fusion), channel_id=1, source_target_pairs={{192,224},{193,225},{194,226},{195,227},{196,228},{197,229},{198,2... | collective-permute-start | bytes 786440 | tf_op jit(solution)/shard_map/ppermute | solution.py:158
  240.6 4.5 %copy-start.1 = (s32[2,1]{0,1:T(1,128)S(1)}, s32[2,1]{0,1:T(1,128)}, u32[]{:S(2)}) copy-start(s32[2,1]{0,1:T(1,128)} %param.26) | copy-start | bytes 28
  (51 other events, 125.9 us)
Sparse Core Ops, SparseCore 0:
  48.3 78.8 all-reduce.1
where the time goes:
time: 253 us; the launch traced here: 252 us
  waiting for transfers between devices  113 us (45%)
  other arithmetic  49.7 us (20%)
  local copies, waits for them, and re-layouts  37.9 us (15%)
  matrix products  19.6 us (8%)
  between operations  18.3 us (7%)
  starting transfers between devices  13.8 us (5%)
    ppermute x10, waiting for transfers between devices, on_device(): got = lax.ppermute(sent, 'ctx', pairs)  62.1 us
    psum x1, waiting for transfers between devices, on_device(): picked = lax.psum(picked, 'ctx')  50.6 us
    unnamed x189, local copies, waits for them, and re-layouts  15.6 us
    convert_element_type x3, other arithmetic, causal_conv(): return jax.nn.silu(total).astype(jnp.bfloat16)  13.1 us
    ppermute x10, starting transfers between devices, on_device(): got = lax.ppermute(sent, 'ctx', pairs)  10.4 us
    dot_general x4, matrix products, block_output(): jnp.einsum('hqs,shp->qhp', weights, x_blk, preferred_element_type=jnp.flo...  7.94 us
    another operation x5, other arithmetic  6.93 us
  transfers between devices with their start and end apart: 15, of which 5 were waited for; matrix products, arithmetic and copies ran while one was open for 25% of the time, Pallas kernels for 0%

commit v1 on v0

--- a/solution.py
+++ b/solution.py
@@ -98,7 +98,9 @@
     conv_pick = jnp.where(on_chip, jnp.where(mine, conv_pool[0], other_conv), 0.0)
     picked = jnp.concatenate([state_pick.reshape(-1), conv_pick.reshape(-1)])
     picked, x_in, bc_in, dt_raw = lax.optimization_barrier((picked, x_in, bc_in, dt_raw))
-    picked = lax.psum(picked, "ctx")
+    picked = picked
+    for hop in (1, 2, 4):
+        picked = picked + lax.ppermute(picked, "ctx", [(dev, dev ^ hop) for dev in range(8)])
     first_state = picked[: state_pick.size].reshape(state_pick.shape)
     first_conv = picked[state_pick.size :].reshape(conv_pick.shape)
     tail_x = x_in[0, tokens - (K - 1) :, :]

time: 253 us -> 279 us (1.10)
  waiting for transfers between devices: 113 us -> 139 us
  between operations: 18.3 us -> 4.82 us
  starting transfers between devices: 13.8 us -> 23.4 us
  other arithmetic: 49.7 us -> 53 us
    ppermute x0 -> x3, waiting for transfers between devices: none -> 85.1 us  [on_device(): lax.ppermute(picked, 'ctx', [(dev, dev ^ hop) for dev in range(8)])]
    psum x1 -> x0, waiting for transfers between devices: 50.6 us -> none  [on_device(): picked = lax.psum(picked, 'ctx')]
    ppermute x0 -> x3, starting transfers between devices: none -> 9.71 us  [on_device(): lax.ppermute(picked, 'ctx', [(dev, dev ^ hop) for dev in range(8)])]
    ppermute x10, waiting for transfers between devices: 62.1 us -> 53.4 us  [on_device(): got = lax.ppermute(sent, 'ctx', pairs)]
    add x0 -> x3, other arithmetic: none -> 2.81 us  [on_device(): picked + lax.ppermute(picked, 'ctx', [(dev, dev ^ hop) for dev in range(8)])]
    unnamed x189 -> x185, local copies, waits for them, and re-layouts: 15.6 us -> 15.1 us
  transfers between devices with their start and end apart: 15 -> 17, of which waited for: 5 -> 6; matrix products, arithmetic and copies ran while one was open for 25% -> 27% of each run, Pallas kernels for 0% -> 0%
where the time goes in v1:
time: 279 us; the launch traced here: 278 us
  waiting for transfers between devices  139 us (50%)
  other arithmetic  53 us (19%)
  local copies, waits for them, and re-layouts  38.9 us (14%)
  starting transfers between devices  23.4 us (8%)
  matrix products  19.5 us (7%)
  between operations  4.82 us (2%)
    ppermute x3, waiting for transfers between devices, on_device(): lax.ppermute(picked, 'ctx', [(dev, dev ^ hop) for dev in range(8)])  85.1 us
    ppermute x10, waiting for transfers between devices, on_device(): got = lax.ppermute(sent, 'ctx', pairs)  53.4 us
    unnamed x185, local copies, waits for them, and re-layouts  15.1 us
    convert_element_type x3, other arithmetic, causal_conv(): return jax.nn.silu(total).astype(jnp.bfloat16)  14.3 us
    ppermute x10, starting transfers between devices, on_device(): got = lax.ppermute(sent, 'ctx', pairs)  10.4 us
    ppermute x3, starting transfers between devices, on_device(): lax.ppermute(picked, 'ctx', [(dev, dev ^ hop) for dev in range(8)])  9.71 us
    dot_general x4, matrix products, block_output(): jnp.einsum('hqs,shp->qhp', weights, x_blk, preferred_element_type=jnp.flo...  7.9 us
    another operation x5, other arithmetic  6.93 us
  transfers between devices with their start and end apart: 17, of which 6 were waited for; matrix products, arithmetic and copies ran while one was open for 27% of the time, Pallas kernels for 0%

profile of v1, /device:TPU:232, one launch (start us, length us, event | category | flops | bytes accessed | tf_op | source)
XLA Modules:
  0.0 278.1 jit_solution(10979423517994858920)
XLA Ops:
  6.5 1.5 fusion.151
  8.0 1.2 fusion.127
  12.4 3.9 %copy.78 = bf16[1,1024,1024]{1,2,0:T(8,128)(2,1)} copy(bf16[1,1024,1024]{2,1,0:T(8,128)(2,1)} %param.16) | data formatting | bytes 4194304 | tf_op args[2]
  18.3 1.3 dynamic-slice_bitcast_fusion.1
  19.6 1.6 slice_bitcast_fusion.3
  21.2 1.3 slice_bitcast_fusion.4
  22.5 2.9 %copy.66 = bf16[1,1024,1024]{1,2,0:T(8,128)(2,1)S(1)} copy(bf16[1,1024,1024]{2,1,0:T(8,128)(2,1)} %param.14) | data formatting | bytes 4194304 | tf_op jit(solution)/shard_map/optimization_barrier | solution.py:100
  25.4 1.3 collective-permute-start.6
  27.0 2.3 reduce-window.14
  35.6 2.6 collective-permute-start.2
  38.2 1.4 collective-permute-start.5
  39.6 3.0 %fusion.21 = f32[1021,1024]{0,1:T(8,128)} fusion(bf16[1,1024,1024]{1,2,0:T(8,128)(2,1)S(1)} %copy.66), kind=kLoop, calls=%fused_computation.38 | loop fusion | flops 1045504 | bytes 6273024 | tf_op jit(solution)/shard_map/convert_element_type | solution.py:24
  44.7 4.5 %reduce-window.16 = f32[16,8,128]{2,1,0:T(8,128)S(1)} reduce-window(f32[16,8,128]{2,1,0:T(8,128)S(1)} %fusion.116, f32[]{:T(128)} %constant.162.clone.1), window={size=1x1x128 pad=0_0x0_0x127_0}, to_apply=%region_3.4 | reduce-window | flops 2080768 | bytes 131076 | tf_op jit(solution)/shard_map/reduce-window.2
  49.6 1.6 maximum_convert_fusion
  51.3 11.2 %multiply_convert_fusion.4 = bf16[1021,1024]{0,1:T(8,128)(2,1)S(1)} fusion(f32[1021,1024]{0,1:T(8,128)} %fusion.21, f32[3,1024]{0,1:T(8,128)} %copy.67, f32[1024]{0:T(1024)S(1)} %bitcast.440, f32[1024]{0:T(1024)S(1)} %bitcast.442, f32[1024]{0:T(1024)S(1)} %bitcast.438, f32[1024]{0:T(1024)S(1)} %bitcast.436), kind=kLoop, calls=%fused_computation.24 | loop fusion | flops 15682560 | bytes 6301696 | tf_op jit(solution)/shard_map/convert_element_type | solution.py:29
  62.5 1.9 fusion.148
  64.5 1.3 add.290
  65.8 2.2 collective-permute-start.3
  72.2 42.2 %collective-permute-done.3 = f32[265216]{0:T(1024)} collective-permute-done((f32[265216]{0:T(1024)S(1)}, f32[265216]{0:T(1024)}, u32[]{:S(2)}, u32[]{:S(2)}) %collective-permute-start.3) | collective-permute-done | bytes 1060896 | tf_op jit(solution)/shard_map/ppermute | solution.py:103
  114.4 1.4 add.291
  115.8 4.9 %collective-permute-start.4 = (f32[265216]{0:T(1024)S(1)}, f32[265216]{0:T(1024)S(1)}, u32[]{:S(2)}, u32[]{:S(2)}) collective-permute-start(f32[265216]{0:T(1024)S(1)} %add.291), channel_id=1, source_target_pairs={{0,128},{32,160},{64,192},{96,224},{128,0},{160,32},{192,64},{224,... | collective-permute-start | bytes 3182600 | tf_op jit(solution)/shard_map/ppermute | solution.py:103
  121.0 2.4 multiply_convert_fusion.9
  124.5 42.9 %collective-permute-done.4 = f32[265216]{0:T(1024)S(1)} collective-permute-done((f32[265216]{0:T(1024)S(1)}, f32[265216]{0:T(1024)S(1)}, u32[]{:S(2)}, u32[]{:S(2)}) %collective-permute-start.4) | collective-permute-done | bytes 1060896 | tf_op jit(solution)/shard_map/ppermute | solution.py:103
  170.1 2.9 %fusion.65 = (bf16[256,1024]{0,1:T(8,128)(2,1)S(1)}, bf16[256,1024]{0,1:T(8,128)(2,1)}, bf16[256,1024]{0,1:T(8,128)(2,1)S(1)}, bf16[256,1024]{0,1:T(8,128)(2,1)S(1)}, bf16[256,1024]{0,1:T(8,128)(2,1)S(1)}) fusion(f32[256,16]{0,1:T(8,128)S(1)} %get-tuple-element.52, bf16[1021,1024]{0,1:T(8,128)(2,1)S(1)} %multiply_convert_fusion.4, ...), kind=kLoop, calls=%fused_computation.94 | loop fusion | flops 4194304 | bytes 6619136 | tf_op jit(solution)/shard_map/convert_element_type | solution.py:38
  173.3 1.3 fusion.85
  174.9 1.3 fusion.79
  176.2 2.5 reshape_reshape.3
  178.8 2.1 multiply_add_fusion
  181.8 1.4 fusion.48
  184.2 2.6 fusion.47
  187.9 2.6 fusion.46
  191.6 1.4 fusion.49
  193.8 1.8 fusion.59
  196.5 1.4 collective-permute-start.12
  197.9 1.7 fusion.58
  199.6 2.5 slice.267
  203.4 1.3 collective-permute-start.13
  206.6 28.6 %collective-permute-done.13 = f32[4,64,256]{2,1,0:T(8,128)S(1)} collective-permute-done((f32[4,64,256]{2,1,0:T(8,128)S(1)}, f32[4,64,256]{2,1,0:T(8,128)S(1)}, u32[]{:S(2)}, u32[]{:S(2)}) %collective-permute-start.13) | collective-permute-done | bytes 262176 | tf_op jit(solution)/shard_map/ppermute | solution.py:160
  236.3 1.8 collective-permute-start.14
  239.1 10.0 %collective-permute-done.14 = f32[4,64,256]{2,1,0:T(8,128)S(1)} collective-permute-done((f32[4,64,256]{2,1,0:T(8,128)S(1)}, f32[4,64,256]{2,1,0:T(8,128)S(1)}, u32[]{:S(2)}, u32[]{:S(2)}) %collective-permute-start.14) | collective-permute-done | bytes 262176 | tf_op jit(solution)/shard_map/ppermute | solution.py:160
  249.2 1.3 collective-permute-start.15
  251.5 7.9 %collective-permute-done.15 = f32[4,64,256]{2,1,0:T(8,128)S(1)} collective-permute-done((f32[4,64,256]{2,1,0:T(8,128)S(1)}, f32[4,64,256]{2,1,0:T(8,128)S(1)}, u32[]{:S(2)}, u32[]{:S(2)}) %collective-permute-start.15) | collective-permute-done | bytes 262176 | tf_op jit(solution)/shard_map/ppermute | solution.py:160
  259.5 1.3 collective-permute-start.16
  260.9 6.9 %collective-permute-done.16 = f32[4,64,256]{2,1,0:T(8,128)S(1)} collective-permute-done((f32[4,64,256]{2,1,0:T(8,128)S(1)}, f32[4,64,256]{2,1,0:T(8,128)S(1)}, u32[]{:S(2)}, u32[]{:S(2)}) %collective-permute-start.16) | collective-permute-done | bytes 262176 | tf_op jit(solution)/shard_map/ppermute | solution.py:160
  268.0 1.6 add_bitcast_fusion
  269.6 1.8 fusion.67
  273.7 1.9 fusion.13
  275.6 2.6 copy.79
  (283 shorter events, 40.1 us)
Async XLA Ops:
  0.6 15.8 %copy-start.28 = (f32[1,16,64,256]{3,2,1,0:T(8,128)S(1)}, f32[1,16,64,256]{3,2,1,0:T(8,128)}, u32[]{:S(2)}) copy-start(f32[1,16,64,256]{3,2,1,0:T(8,128)} %param.23) | copy-start | bytes 3145732
  0.7 15.7 %copy-start.36 = (f32[1,3,1024]{2,0,1:T(1,128)S(1)}, f32[1,3,1024]{2,0,1:T(1,128)}, u32[]{:S(2)}) copy-start(f32[1,3,1024]{2,0,1:T(1,128)} %param.24) | copy-start | bytes 36868
  0.7 15.8 %collective-permute-start = (f32[16,64,256]{2,1,0:T(8,128)}, f32[16,64,256]{2,1,0:T(8,128)S(1)}, u32[]{:S(2)}, u32[]{:S(2)}) collective-permute-start(f32[16,64,256]{2,1,0:T(8,128)} %bitcast.416), channel_id=1, source_target_pairs={{0,1},{1,0},{2,3},{3,2},{4,5},{5,4},{6,7},{7,6},{8,9},{9,8},{10,11... | collective-permute-start | bytes 3145736 | tf_op jit(solution)/shard_map/ppermute | solution.py:96
  1.5 14.9 %collective-permute-start.1 = (f32[3,1024]{1,0:T(4,128)S(1)}, f32[3,1024]{1,0:T(4,128)S(1)}, u32[]{:S(2)}, u32[]{:S(2)}) collective-permute-start(f32[3,1024]{1,0:T(4,128)S(1)} %bitcast.445), channel_id=1, source_target_pairs={{0,1},{1,0},{2,3},{3,2},{4,5},{5,4},{6,7},{7,6},{8,9},{9,8},{10,11... | collective-permute-start | bytes 36872 | tf_op jit(solution)/shard_map/ppermute | solution.py:96
  17.2 9.6 %copy-start.62 = (f32[16]{0:T(128)S(1)}, f32[16]{0:T(128)}, u32[]{:S(2)}) copy-start(f32[16]{0:T(128)} %param.18) | copy-start | bytes 196
  17.2 9.6 %copy-start.64 = (f32[16]{0:T(128)S(1)}, f32[16]{0:T(128)}, u32[]{:S(2)}) copy-start(f32[16]{0:T(128)} %param.19) | copy-start | bytes 196
  19.6 30.0 %copy-start.11 = (bf16[1024,256]{1,0:T(8,128)(2,1)}, bf16[1024,256]{1,0:T(8,128)(2,1)S(1)}, u32[]{:S(2)}) copy-start(bf16[1024,256]{1,0:T(8,128)(2,1)S(1)} %get-tuple-element.27) | copy-start | bytes 1572868
  19.6 30.0 %copy-start.12 = (bf16[1024,256]{1,0:T(8,128)(2,1)}, bf16[1024,256]{1,0:T(8,128)(2,1)S(1)}, u32[]{:S(2)}) copy-start(bf16[1024,256]{1,0:T(8,128)(2,1)S(1)} %get-tuple-element.28) | copy-start | bytes 1572868
  25.4 45.9 %collective-permute-start.6 = (bf16[3,4096]{1,0:T(4,128)(2,1)}, bf16[3,4096]{1,0:T(4,128)(2,1)}, u32[]{:S(2)}, u32[]{:S(2)}) collective-permute-start(bf16[3,4096]{1,0:T(4,128)(2,1)} %slice_bitcast_fusion.3), channel_id=1, source_target_pairs={{0,32},{32,64},{64,96},{96,128},{128,160},{160,192},{192,224},{1,3... | collective-permute-start | bytes 73736 | tf_op jit(solution)/shard_map/ppermute | solution.py:20
  29.3 14.4 %copy-start.63 = (f32[16]{0:T(128)S(1)}, f32[16]{0:T(128)}, u32[]{:S(2)}) copy-start(f32[16]{0:T(128)} %param.18) | copy-start | bytes 196
  29.3 14.4 %copy-start.65 = (f32[16]{0:T(128)S(1)}, f32[16]{0:T(128)}, u32[]{:S(2)}) copy-start(f32[16]{0:T(128)} %param.19) | copy-start | bytes 196
  29.3 15.2 %copy-start.48 = (f32[8,128]{1,0:T(8,128)S(1)}, f32[8,128]{1,0:T(8,128)}, u32[]{:S(2)}) copy-start(f32[8,128]{1,0:T(8,128)} %fusion.127) | copy-start | bytes 12292
  35.6 28.9 %collective-permute-start.2 = (f32[265216]{0:T(1024)}, f32[265216]{0:T(1024)}, u32[]{:S(2)}, u32[]{:S(2)}) collective-permute-start(f32[265216]{0:T(1024)} %pad_maximum_fusion.2), channel_id=1, source_target_pairs={{0,32},{32,0},{64,96},{96,64},{128,160},{160,128},{192,224},{224,1... | collective-permute-start | bytes 3182600 | tf_op jit(solution)/shard_map/ppermute | solution.py:103
  38.2 13.0 %copy-start.46 = (f32[1,1024]{1,0:T(1,128)S(1)}, f32[1,1024]{1,0:T(1,128)}, u32[]{:S(2)}) copy-start(f32[1,1024]{1,0:T(1,128)} %get-tuple-element.61) | copy-start | bytes 12292
  38.2 13.0 %copy-start.47 = (f32[1,1024]{1,0:T(1,128)S(1)}, f32[1,1024]{1,0:T(1,128)}, u32[]{:S(2)}) copy-start(f32[1,1024]{1,0:T(1,128)} %get-tuple-element.62) | copy-start | bytes 12292
  38.2 130.3 %collective-permute-start.5 = (bf16[3,1024]{1,0:T(4,128)(2,1)}, bf16[3,1024]{1,0:T(4,128)(2,1)S(1)}, u32[]{:S(2)}, u32[]{:S(2)}) collective-permute-start(bf16[3,1024]{1,0:T(4,128)(2,1)} %get-tuple-element.35), channel_id=1, source_target_pairs={{0,32},{32,64},{64,96},{96,128},{128,160},{160,192},{192,224},{1,3... | collective-permute-start | bytes 18440 | tf_op jit(solution)/shard_map/ppermute | solution.py:20
  44.4 18.1 %copy-start.66 = (f32[16]{0:T(128)}, f32[16]{0:T(128)S(1)}, u32[]{:S(2)}) copy-start(f32[16]{0:T(128)S(1)} %get-tuple-element.85) | copy-start | bytes 196
  51.3 13.2 %copy-start.13 = (f32[265216]{0:T(1024)S(1)}, f32[265216]{0:T(1024)}, u32[]{:S(2)}) copy-start(f32[265216]{0:T(1024)} %pad_maximum_fusion.2) | copy-start | bytes 3182596
  65.8 55.2 %copy-start.57 = (f32[1,512]{1,0:T(1,128)S(1)}, f32[1,512]{1,0:T(1,128)}, u32[]{:S(2)}) copy-start(f32[1,512]{1,0:T(1,128)} %get-tuple-element.63) | copy-start | bytes 6148
  65.8 55.2 %copy-start.58 = (f32[1,512]{1,0:T(1,128)S(1)}, f32[1,512]{1,0:T(1,128)}, u32[]{:S(2)}) copy-start(f32[1,512]{1,0:T(1,128)} %get-tuple-element.64) | copy-start | bytes 6148
  65.8 55.2 %copy-start.59 = (f32[1,512]{1,0:T(1,128)S(1)}, f32[1,512]{1,0:T(1,128)}, u32[]{:S(2)}) copy-start(f32[1,512]{1,0:T(1,128)} %get-tuple-element.65) | copy-start | bytes 6148
  65.8 55.2 %copy-start.60 = (f32[1,512]{1,0:T(1,128)S(1)}, f32[1,512]{1,0:T(1,128)}, u32[]{:S(2)}) copy-start(f32[1,512]{1,0:T(1,128)} %get-tuple-element.66) | copy-start | bytes 6148
  65.8 48.6 %collective-permute-start.3 = (f32[265216]{0:T(1024)S(1)}, f32[265216]{0:T(1024)}, u32[]{:S(2)}, u32[]{:S(2)}) collective-permute-start(f32[265216]{0:T(1024)S(1)} %add.290), channel_id=1, source_target_pairs={{0,64},{32,96},{64,0},{96,32},{128,192},{160,224},{192,128},{224,1... | collective-permute-start | bytes 3182600 | tf_op jit(solution)/shard_map/ppermute | solution.py:103
  71.2 49.5 %copy-start.9 = (f32[1024,512]{1,0:T(8,128)S(1)}, f32[1024,512]{1,0:T(8,128)}, u32[]{:S(2)}) copy-start(f32[1024,512]{1,0:T(8,128)} %maximum_convert_fusion) | copy-start | bytes 6291460
  115.8 51.5 %collective-permute-start.4 = (f32[265216]{0:T(1024)S(1)}, f32[265216]{0:T(1024)S(1)}, u32[]{:S(2)}, u32[]{:S(2)}) collective-permute-start(f32[265216]{0:T(1024)S(1)} %add.291), channel_id=1, source_target_pairs={{0,128},{32,160},{64,192},{96,224},{128,0},{160,32},{192,64},{224,... | collective-permute-start | bytes 3182600 | tf_op jit(solution)/shard_map/ppermute | solution.py:103
  123.4 51.5 %copy-start.4 = (bf16[1024,512]{1,0:T(8,128)(2,1)}, bf16[1024,512]{1,0:T(8,128)(2,1)S(1)}, u32[]{:S(2)}) copy-start(bf16[1024,512]{1,0:T(8,128)(2,1)S(1)} %multiply_convert_fusion.9) | copy-start | bytes 3145732
  181.0 2.4 collective-permute-start.7
  183.5 3.5 %collective-permute-start.8 = (f32[4,64,256]{2,1,0:T(8,128)S(1)}, f32[4,64,256]{2,1,0:T(8,128)S(1)}, u32[]{:S(2)}, u32[]{:S(2)}) collective-permute-start(f32[4,64,256]{2,1,0:T(8,128)S(1)} %bitcast_add_fusion.8), channel_id=1, source_target_pairs={{0,32},{32,64},{1,33},{33,65},{2,34},{34,66},{3,35},{35,67},{4,36}... | collective-permute-start | bytes 786440 | tf_op jit(solution)/shard_map/ppermute | solution.py:160
  187.1 3.5 %collective-permute-start.9 = (f32[4,64,256]{2,1,0:T(8,128)S(1)}, f32[4,64,256]{2,1,0:T(8,128)S(1)}, u32[]{:S(2)}, u32[]{:S(2)}) collective-permute-start(f32[4,64,256]{2,1,0:T(8,128)S(1)} %bitcast_add_fusion.7), channel_id=1, source_target_pairs={{0,32},{32,64},{64,96},{1,33},{33,65},{65,97},{2,34},{34,66},{66,9... | collective-permute-start | bytes 786440 | tf_op jit(solution)/shard_map/ppermute | solution.py:160
  190.8 2.2 collective-permute-start.10
  193.1 2.5 collective-permute-start.11
  195.7 39.5 %copy-start.72 = (f32[4]{0:T(128)S(1)}, f32[4]{0:T(128)}, u32[]{:S(2)}) copy-start(f32[4]{0:T(128)} %get-tuple-element.69) | copy-start | bytes 52
  196.5 5.7 %collective-permute-start.12 = (f32[4,64,256]{2,1,0:T(8,128)}, f32[4,64,256]{2,1,0:T(8,128)}, u32[]{:S(2)}, u32[]{:S(2)}) collective-permute-start(f32[4,64,256]{2,1,0:T(8,128)} %bitcast_add_fusion.4), channel_id=1, source_target_pairs={{64,96},{96,128},{128,160},{160,192},{65,97},{97,129},{129,161},{1... | collective-permute-start | bytes 786440 | tf_op jit(solution)/shard_map/ppermute | solution.py:160
  197.9 51.3 %copy-start.71 = (f32[4]{0:T(128)S(1)}, f32[4]{0:T(128)}, u32[]{:S(2)}) copy-start(f32[4]{0:T(128)} %get-tuple-element.68) | copy-start | bytes 52
  199.6 59.9 %copy-start.70 = (f32[4]{0:T(128)S(1)}, f32[4]{0:T(128)}, u32[]{:S(2)}) copy-start(f32[4]{0:T(128)} %get-tuple-element.67) | copy-start | bytes 52
  202.1 37.0 %copy-start.27 = (f32[4,64,256]{2,1,0:T(8,128)S(1)}, f32[4,64,256]{2,1,0:T(8,128)}, u32[]{:S(2)}) copy-start(f32[4,64,256]{2,1,0:T(8,128)} %copy-done.26) | copy-start | bytes 786436
  202.1 47.0 %copy-start.3 = (f32[4,4,64,256]{3,2,1,0:T(8,128)S(1)}, f32[4,4,64,256]{3,2,1,0:T(8,128)}, u32[]{:S(2)}) copy-start(f32[4,4,64,256]{3,2,1,0:T(8,128)} %reshape_reshape.3) | copy-start | bytes 3145732
  203.4 31.8 %collective-permute-start.13 = (f32[4,64,256]{2,1,0:T(8,128)S(1)}, f32[4,64,256]{2,1,0:T(8,128)S(1)}, u32[]{:S(2)}, u32[]{:S(2)}) collective-permute-start(f32[4,64,256]{2,1,0:T(8,128)S(1)} %bitcast_add_fusion.3), channel_id=1, source_target_pairs={{96,128},{128,160},{160,192},{192,224},{97,129},{129,161},{161,193... | collective-permute-start | bytes 786440 | tf_op jit(solution)/shard_map/ppermute | solution.py:160
  236.2 31.7 %copy-start.7 = (f32[16,64,256]{2,1,0:T(8,128)S(1)}, f32[16,64,256]{2,1,0:T(8,128)}, u32[]{:S(2)}) copy-start(f32[16,64,256]{2,1,0:T(8,128)} %fusion.85) | copy-start | bytes 3145732
  236.2 31.7 %copy-start.8 = (f32[16,64,256]{2,1,0:T(8,128)S(1)}, f32[16,64,256]{2,1,0:T(8,128)}, u32[]{:S(2)}) copy-start(f32[16,64,256]{2,1,0:T(8,128)} %fusion.79) | copy-start | bytes 3145732
  236.3 31.7 %copy-start.16 = (f32[16,64,256]{2,1,0:T(8,128)S(1)}, f32[16,64,256]{2,1,0:T(8,128)}, u32[]{:S(2)}) copy-start(f32[16,64,256]{2,1,0:T(8,128)} %slice.267) | copy-start | bytes 3145732
  236.3 31.7 %copy-start.67 = (f32[16]{0:T(128)S(1)}, f32[16]{0:T(128)}, u32[]{:S(2)}) copy-start(f32[16]{0:T(128)} %copy-done.66) | copy-start | bytes 196
  236.3 31.7 %copy-start.68 = (f32[16]{0:T(128)S(1)}, f32[16]{0:T(128)}, u32[]{:S(2)}) copy-start(f32[16]{0:T(128)} %get-tuple-element.86) | copy-start | bytes 196
  236.3 31.7 %copy-start.79 = (f32[16]{0:T(128)S(1)}, f32[16]{0:T(128)}, u32[]{:S(2)}) copy-start(f32[16]{0:T(128)} %get-tuple-element.83) | copy-start | bytes 196
  236.3 31.7 %copy-start.80 = (f32[16]{0:T(128)S(1)}, f32[16]{0:T(128)}, u32[]{:S(2)}) copy-start(f32[16]{0:T(128)} %get-tuple-element.84) | copy-start | bytes 196
  236.3 12.8 %collective-permute-start.14 = (f32[4,64,256]{2,1,0:T(8,128)S(1)}, f32[4,64,256]{2,1,0:T(8,128)S(1)}, u32[]{:S(2)}, u32[]{:S(2)}) collective-permute-start(f32[4,64,256]{2,1,0:T(8,128)S(1)} %bitcast_add_fusion.2), channel_id=1, source_target_pairs={{128,160},{160,192},{192,224},{129,161},{161,193},{193,225},{130,1... | collective-permute-start | bytes 786440 | tf_op jit(solution)/shard_map/ppermute | solution.py:160
  249.2 10.2 %collective-permute-start.15 = (f32[4,64,256]{2,1,0:T(8,128)S(1)}, f32[4,64,256]{2,1,0:T(8,128)S(1)}, u32[]{:S(2)}, u32[]{:S(2)}) collective-permute-start(f32[4,64,256]{2,1,0:T(8,128)S(1)} %bitcast_add_fusion.1), channel_id=1, source_target_pairs={{160,192},{192,224},{161,193},{193,225},{162,194},{194,226},{163,1... | collective-permute-start | bytes 786440 | tf_op jit(solution)/shard_map/ppermute | solution.py:160
  259.5 8.3 %collective-permute-start.16 = (f32[4,64,256]{2,1,0:T(8,128)S(1)}, f32[4,64,256]{2,1,0:T(8,128)S(1)}, u32[]{:S(2)}, u32[]{:S(2)}) collective-permute-start(f32[4,64,256]{2,1,0:T(8,128)S(1)} %bitcast_add_fusion), channel_id=1, source_target_pairs={{192,224},{193,225},{194,226},{195,227},{196,228},{197,229},{198,2... | collective-permute-start | bytes 786440 | tf_op jit(solution)/shard_map/ppermute | solution.py:160
  (51 other events, 169.3 us)
